TPU v7x, 128 devices: a whole 4x4x4 slice. The times are simulated.
128 devices in a mesh: seq: 32 (over z, y, core), tp: 4 (over x).
Axes of the slice: x: 4, y: 4, z: 4, core: 2. Of those that a mesh axis runs over, the one named last changes fastest.
Arguments:
- tokens: bfloat16 [16384, 1408], P('seq'), may hold values from -70 to 70
- group_image: int32 [4096], P('seq'), may hold values from 0 to 31, never falling along the last dimension, each value on 1 to 512 neighbouring positions
- image_slot: int32 [32], replicated, may hold values from 0 to 31, each once
- attention_gain: float32 [1408], replicated, may hold values from 0.1 to 1.9
- query_weight: bfloat16 [1408, 1408], P(None, 'tp'), may hold values from -1.11930376 to 1.11930376
- key_weight: bfloat16 [1408, 1408], P(None, 'tp'), may hold values from -1.11930376 to 1.11930376
- value_weight: bfloat16 [1408, 1408], P(None, 'tp'), may hold values from -1.25 to 1.25
- output_weight: bfloat16 [1408, 1408], P('tp'), may hold values from -0.15625 to 0.15625
- feedforward_gain: float32 [1408], replicated, may hold values from 0.1 to 1.9
- up_weight: bfloat16 [1408, 6144], P(None, 'tp'), may hold values from -0.15625 to 0.15625
- down_weight: bfloat16 [6144, 1408], P('tp'), may hold values from -0.078125 to 0.078125
- merge_gain: float32 [1408], replicated, may hold values from 0.1 to 1.9
- merge_weight: bfloat16 [5632, 3584], P(None, 'tp'), may hold values from -0.078125 to 0.078125
Outputs:
- merged_rows: bfloat16 [32, 512, 3584], P('seq', None, 'tp')
Inputs may be any that keep to these rules, and one draw needn't show every extreme that they name: `group_image`: images are numbered in the order of their groups, each covers consecutive groups, 1 to 512 of them, and one covers exactly 512.
All inputs are finite; a program needn't handle non-finite values.
Results may differ from a plain program's by a relative error of at most 0.012.
Values may be sent and summed in bfloat16 or wider, within the bound.
No kernel may reach another device: no remote copies, remote signals or barrier semaphores. Data moves between devices by JAX's collectives and lax.ppermute only.
A program may use at most 192 MiB of HBM per device.

v0:
```python
import jax
import jax.numpy as jnp
from jax import lax
from jax.sharding import PartitionSpec as P

D = 1408
HD = 88
REACH = 4
epsilon = 1e-06
masked_score = -1e30


def shifted(value, axis, steps):
    count = lax.axis_size(axis)
    initial, last = (max(0, -steps), min(count, count - steps))
    return lax.ppermute(value, axis, [(source, source + steps) for source in range(initial, last)])


def finish_norm(hidden, row_mean, square, norm_gain):
    return (
        (hidden - row_mean) * lax.rsqrt(square - row_mean * row_mean + epsilon) * norm_gain
    ).astype(jnp.bfloat16)


def full_norm(hidden, norm_gain):
    row_mean = jnp.mean(hidden, axis=1, keepdims=True)
    square = jnp.mean(hidden * hidden, axis=1, keepdims=True)
    return finish_norm(hidden, row_mean, square, norm_gain)


def sum_rows(partial_value):
    return lax.psum(partial_value, "tp")


def attend_window(query_heads, key_heads, value_heads, query_image, key_image):
    scores = jnp.einsum(
        "qhd,khd->hqk", query_heads, key_heads, preferred_element_type=jnp.float32
    ) * HD ** (-0.5)
    same_image = query_image[:, None] == key_image[None, :]
    scores = jnp.where(same_image[None], scores, masked_score)
    row_best = jnp.max(scores, axis=2, keepdims=True)
    weights = jnp.exp(scores - row_best)
    row_total = jnp.sum(weights, axis=2)
    weighted = jnp.einsum(
        "hqk,khd->qhd",
        weights.astype(jnp.bfloat16),
        value_heads,
        preferred_element_type=jnp.float32,
    )
    return weighted / jnp.transpose(row_total)[:, :, None]


def image_of_groups(groups, starts, group_total):
    inside = (groups >= 0) & (groups < group_total)
    image = jnp.sum((starts[None, :] <= groups[:, None]).astype(jnp.int32), axis=1) - 1
    return jnp.where(inside, image, -1)


def route_to_owners(projected, starts, counts, image_slot, device, seq_count):
    group_rows, out_cols = projected.shape
    per_pair = group_rows // seq_count
    spread = projected.reshape(per_pair, seq_count, out_cols).transpose(1, 0, 2)
    spread = lax.all_to_all(spread, "seq", split_axis=0, concat_axis=0, tiled=True)
    held = spread.reshape(group_rows, out_cols)
    image_count = image_slot.shape[0]
    most_rows = REACH * group_rows
    per_owner = most_rows // seq_count
    image_ids = jnp.arange(image_count, dtype=jnp.int32)
    owners = jnp.arange(seq_count, dtype=jnp.int32)
    owned_image = jnp.sum(
        jnp.where(image_slot[None, :] == owners[:, None], image_ids[None, :], 0), axis=1
    )
    owner_start = starts[owned_image]
    owner_count = counts[owned_image]
    first_pos = jnp.mod(device - owner_start, seq_count)
    first_row = (owner_start + first_pos - device) // seq_count
    steps = jnp.arange(per_owner, dtype=jnp.int32)
    rows = first_row[:, None] + steps[None, :]
    valid = first_pos[:, None] + seq_count * steps[None, :] < owner_count[:, None]
    rows = jnp.clip(rows, 0, group_rows - 1)
    outgoing = jnp.take(held, rows.reshape(-1), axis=0).reshape(seq_count, per_owner, out_cols)
    outgoing = jnp.where(valid[:, :, None], outgoing, jnp.zeros((), outgoing.dtype))
    received = lax.all_to_all(outgoing, "seq", split_axis=0, concat_axis=0, tiled=True)
    own_image = jnp.sum(jnp.where(image_slot == device, image_ids, 0))
    own_start = starts[own_image]
    order = jnp.mod(own_start + jnp.arange(seq_count, dtype=jnp.int32), seq_count)
    placed = jnp.take(received, order, axis=0).transpose(1, 0, 2)
    return placed.reshape(most_rows, out_cols)


def shards(
    tokens,
    group_image,
    image_slot,
    attention_gain,
    query_weight,
    key_weight,
    value_weight,
    output_weight,
    feedforward_gain,
    up_weight,
    down_weight,
    merge_gain,
    merge_weight,
):
    device = lax.axis_index("seq")
    seq_count = lax.axis_size("seq")
    token_rows = tokens.shape[0]
    group_rows = group_image.shape[0]
    group_total = group_rows * seq_count
    image_count = image_slot.shape[0]
    image_ids = jnp.arange(image_count, dtype=jnp.int32)
    local_counts = jnp.sum((group_image[:, None] == image_ids[None, :]).astype(jnp.int32), axis=0)
    counts = lax.psum(local_counts, "seq")
    starts = jnp.cumsum(counts) - counts
    query_image = jnp.repeat(group_image, 4)
    residual = tokens.astype(jnp.float32)
    normed = full_norm(residual, attention_gain)
    head_count = query_weight.shape[1] // HD
    queries = jnp.dot(normed, query_weight, preferred_element_type=jnp.float32).astype(jnp.bfloat16)
    key_rows = jnp.dot(normed, key_weight, preferred_element_type=jnp.float32).astype(jnp.bfloat16)
    value_rows = jnp.dot(normed, value_weight, preferred_element_type=jnp.float32).astype(
        jnp.bfloat16
    )
    query_heads = queries.reshape(token_rows, head_count, HD)
    key_value = jnp.stack([key_rows, value_rows])
    arrived = []
    for offset in range(REACH, -REACH - 1, -1):
        if offset == 0:
            arrived.append(key_value)
        else:
            arrived.append(shifted(key_value, "seq", offset))
    window = jnp.concatenate(arrived, axis=1)
    window_groups = (device - REACH) * group_rows + jnp.arange(
        (2 * REACH + 1) * group_rows, dtype=jnp.int32
    )
    key_image = jnp.repeat(image_of_groups(window_groups, starts, group_total), 4)
    context = attend_window(
        query_heads,
        window[0].reshape(-1, head_count, HD),
        window[1].reshape(-1, head_count, HD),
        query_image,
        key_image,
    )
    context = context.astype(jnp.bfloat16).reshape(token_rows, head_count * HD)
    attention_part = jnp.dot(context, output_weight, preferred_element_type=jnp.float32)
    after_attention = residual + sum_rows(attention_part)
    normed_two = full_norm(after_attention, feedforward_gain)
    hidden_units = jax.nn.gelu(
        jnp.dot(normed_two, up_weight, preferred_element_type=jnp.float32), approximate=False
    ).astype(jnp.bfloat16)
    after_feedforward = after_attention + sum_rows(
        jnp.dot(hidden_units, down_weight, preferred_element_type=jnp.float32)
    )
    normed_three = full_norm(after_feedforward, merge_gain)
    grouped = normed_three.reshape(group_rows, 4 * D)
    projected = jnp.dot(grouped, merge_weight, preferred_element_type=jnp.float32).astype(
        jnp.bfloat16
    )
    return route_to_owners(projected, starts, counts, image_slot, device, seq_count)[None]


def solution(mesh):
    return jax.shard_map(
        shards,
        mesh=mesh,
        in_specs=(
            P("seq", None),
            P("seq"),
            P(),
            P(),
            P(None, "tp"),
            P(None, "tp"),
            P(None, "tp"),
            P("tp", None),
            P(),
            P(None, "tp"),
            P("tp", None),
            P(),
            P(None, "tp"),
        ),
        out_specs=P("seq", None, "tp"),
        check_vma=False,
    )
```

profile of v0, /device:TPU:1, one launch (start us, length us, event | category | flops | bytes accessed | tf_op | source)
XLA Modules:
  0.0 418.6 jit_solution(13911761281440724261)
XLA Ops:
  6.5 2.0 convert_reduce_fusion
  8.6 1.9 fusion.18
  13.9 6.5 %collective-permute-start = (bf16[2,512,352]{1,2,0:T(8,128)(2,1)}, bf16[2,512,352]{1,2,0:T(8,128)(2,1)}, u32[]{:S(2)}, u32[]{:S(2)}) collective-permute-start(bf16[2,512,352]{1,2,0:T(8,128)(2,1)} %pad_maximum_fusion), channel_id=1, source_target_pairs={{0,16},{4,20},{8,24},{12,28},{16,32},{20,36},{24,40},{28,44},{32,4... | collective-permute-start | bytes 2162696 | tf_op jit(solution)/shard_map/ppermute | solution.py:16
  20.5 4.1 collective-permute-start.1
  24.6 3.2 collective-permute-start.2
  27.9 1.9 collective-permute-start.3
  29.8 3.2 collective-permute-start.4
  33.2 47.7 %psum.21 = s32[32]{0:T(128)S(1)} all-reduce(s32[32]{0:T(128)S(1)} %convert_reduce_fusion.2), channel_id=1, replica_groups=mesh['seq'=32,'tp'=4] {'seq'}, use_global_device_ids=true, to_apply=%region_1.0 | all-reduce | flops 32 | bytes 256 | tf_op jit(solution)/shard_map/psum | solution.py:114
  83.3 2.4 convolution_convert_fusion
  85.8 1.4 collective-permute-start.5
  90.8 1.5 collective-permute-start.7
  95.9 7.1 %collective-permute-done.5 = bf16[2,512,352]{1,2,0:T(8,128)(2,1)S(1)} collective-permute-done((bf16[2,512,352]{1,2,0:T(8,128)(2,1)}, bf16[2,512,352]{1,2,0:T(8,128)(2,1)S(1)}, u32[]{:S(2)}, u32[]{:S(2)}) %collective-permute-start.5) | collective-permute-done | bytes 720928 | tf_op jit(solution)/shard_map/ppermute | solution.py:16
  103.0 2.5 collective-permute-done.6
  105.5 10.1 %collective-permute-done.7 = bf16[2,512,352]{1,2,0:T(8,128)(2,1)S(1)} collective-permute-done((bf16[2,512,352]{1,2,0:T(8,128)(2,1)}, bf16[2,512,352]{1,2,0:T(8,128)(2,1)S(1)}, u32[]{:S(2)}, u32[]{:S(2)}) %collective-permute-start.7) | collective-permute-done | bytes 720928 | tf_op jit(solution)/shard_map/ppermute | solution.py:16
  115.7 3.1 fusion.112
  118.8 18.3 %fusion = (f32[4,512]{1,0:T(4,128)S(1)}, f32[4,512,4608]{2,1,0:T(8,128)}) fusion(pred[512,4608]{1,0:T(8,128)(4,1)S(1)} %broadcast_compare_fusion, bf16[512,4,88]{0,2,1:T(8,128)(2,1)S(1)} %bitcast.55, bf16[4608,4,88]{0,2,1:T(8,128)(2,1)} %bitcast.50), kind=kOutput, calls=%fused_computation.6 | convolution fusion | flops 1689253888 | bytes 43720704 | tf_op jit(solution)/shard_map/qhd,khd->hqk/dot_general | solution.py:36
  137.1 17.4 %fusion.1 = f32[4,512]{1,0:T(4,128)S(1)} fusion(f32[4,512,4608]{2,1,0:T(8,128)} %get-tuple-element.23, f32[4,512]{1,0:T(4,128)S(1)} %get-tuple-element.22, pred[512,4608]{1,0:T(8,128)(4,1)S(1)} %broadcast_compare_fusion), kind=kLoop, calls=%fused_computation.7 | loop fusion | flops 37746688 | bytes 40124416 | tf_op jit(solution)/shard_map/reduce_sum | solution.py:43
  154.6 15.3 %fusion.67 = bf16[512,4,88]{0,2,1:T(8,128)(2,1)S(1)} fusion(bf16[4608,4,88]{0,2,1:T(8,128)(2,1)S(1)} %bitcast.49, f32[4,512,4608]{2,1,0:T(8,128)} %get-tuple-element.23, f32[4,512]{1,0:T(4,128)S(1)} %get-tuple-element.22, pred[512,4608]{1,0:T(8,128)(4,1)S(1)} %broadcast_compare_fusion, f32[512,4]{0,1:T(4,128)S(1)} %bitcast.53), kind=kOutput, calls=%fused_computation.86 | convolution fusion | flops 1699053568 | bytes 43728896 | tf_op jit(solution)/shard_map/hqk,khd->qhd/dot_general | solution.py:44
  169.9 2.6 fusion.113
  172.8 93.7 %all-reduce.3.cloned.1.call-done = f32[512,1408]{1,0:T(8,128)} async-done(((f32[512,1408]{1,0:T(8,128)}), f32[512,1408]{1,0:T(8,128)}) %all-reduce.3.cloned.1.call-update) | async-done | bytes 2883600 | tf_op jit(solution)/shard_map/psum | solution.py:32
  266.5 2.4 fusion.71
  268.9 16.2 %fusion.20 = f32[512,1408]{1,0:T(8,128)} fusion(bf16[1536,1408]{1,0:T(8,128)(2,1)} %param.23, bf16[1408,1536]{1,0:T(8,128)(2,1)} %param.22, f32[1408]{0:T(1024)S(1)} %copy-done.13, f32[512]{0:T(512)S(1)} %get-tuple-element.19, f32[512]{0:T(512)S(1)} %get-tuple-element.18, f32[512,1408]{1,0:T(8,128)} %all-reduce.3.cloned.1.call-done, ...), kind=kOutput, calls=%fused_computation.43 | convolution fusion | flops 4484628480 | bytes 15869440 | tf_op jit(solution)/shard_map/dot_general | solution.py:153
  286.9 69.7 %all-reduce.5.cloned.1.call-done = f32[512,1408]{1,0:T(8,128)} async-done(((f32[512,1408]{1,0:T(8,128)}), f32[512,1408]{1,0:T(8,128)}) %all-reduce.5.cloned.1.call-update) | async-done | bytes 2883600 | tf_op jit(solution)/shard_map/psum | solution.py:32
  356.6 3.3 fusion.110
  359.9 1.6 multiply_convert_fusion
  361.5 2.7 reshape.342
  364.2 5.6 %convolution_convert_fusion.3 = bf16[128,896]{1,0:T(8,128)(2,1)S(1)} fusion(bf16[128,5632]{1,0:T(8,128)(2,1)S(1)} %reshape.342, bf16[5632,896]{1,0:T(8,128)(2,1)} %param.25), kind=kOutput, calls=%fused_computation.84 | convolution fusion | flops 1291960320 | bytes 11763712 | tf_op jit(solution)/shard_map/dot_general | solution.py:157
  370.6 7.7 %all-to-all-start = ((bf16[32,4,896]{2,1,0:T(4,128)(2,1)}), bf16[32,4,896]{2,1,0:T(4,128)(2,1)S(1)}, u32[]{:S(2)}, u32[]{:S(2)}) async-start(bf16[32,4,896]{2,1,0:T(4,128)(2,1)} %bitcast.46), calls=%async_computation | async-start | bytes 458752 | tf_op jit(solution)/shard_map/all_to_all | solution.py:63
  378.4 8.5 %all-to-all-done = bf16[32,4,896]{2,1,0:T(4,128)(2,1)S(1)} async-done(((bf16[32,4,896]{2,1,0:T(4,128)(2,1)}), bf16[32,4,896]{2,1,0:T(4,128)(2,1)S(1)}, u32[]{:S(2)}, u32[]{:S(2)}) %all-to-all-start) | async-done | bytes 229408 | tf_op jit(solution)/shard_map/all_to_all | solution.py:63
  386.9 2.1 gather_fusion.2
  390.2 3.8 all-to-all-start.1
  398.8 11.0 %all-to-all-done.1 = bf16[32,16,896]{2,1,0:T(8,128)(2,1)S(1)} async-done(((bf16[32,16,896]{2,1,0:T(8,128)(2,1)}), bf16[32,16,896]{2,1,0:T(8,128)(2,1)S(1)}, u32[]{:S(2)}, u32[]{:S(2)}) %all-to-all-start.1) | async-done | bytes 917536 | tf_op jit(solution)/shard_map/all_to_all | solution.py:83
  (91 shorter events, 22.2 us)
Async XLA Ops:
  6.5 163.3 %copy-start = (bf16[352,1408]{1,0:T(8,128)(2,1)S(1)}, bf16[352,1408]{1,0:T(8,128)(2,1)}, u32[]{:S(2)}) copy-start(bf16[352,1408]{1,0:T(8,128)(2,1)} %param.20) | copy-start | bytes 2973700
  6.5 3.9 copy-start.11
  6.5 259.9 %all-reduce.3.cloned.1.call-start = ((), (), s32[]{:S(2)}) async-start(), calls=%async_computation.2 | async-start | bytes 5767168 | tf_op jit(solution)/shard_map/psum | solution.py:32
  10.5 2.5 copy-start.4
  10.5 1.7 copy-start.12
  12.2 1.8 copy-start.5
  12.2 20.9 %copy-start.10 = (s32[128]{0:T(128)S(1)}, s32[128]{0:T(128)}, u32[]{:S(2)}) copy-start(s32[128]{0:T(128)} %param.14) | copy-start | bytes 1540
  13.0 7.5 %copy-start.7 = (bf16[1,512,352]{1,2,0:T(8,128)(2,1)}, bf16[1,512,352]{1,2,0:T(8,128)(2,1)S(1)}, u32[]{:S(2)}) copy-start(bf16[1,512,352]{1,2,0:T(8,128)(2,1)S(1)} %fusion.62) | copy-start | bytes 1081348
  13.9 71.8 %collective-permute-start = (bf16[2,512,352]{1,2,0:T(8,128)(2,1)}, bf16[2,512,352]{1,2,0:T(8,128)(2,1)}, u32[]{:S(2)}, u32[]{:S(2)}) collective-permute-start(bf16[2,512,352]{1,2,0:T(8,128)(2,1)} %pad_maximum_fusion), channel_id=1, source_target_pairs={{0,16},{4,20},{8,24},{12,28},{16,32},{20,36},{24,40},{28,44},{32,4... | collective-permute-start | bytes 2162696 | tf_op jit(solution)/shard_map/ppermute | solution.py:16
  20.5 67.9 %collective-permute-start.1 = (bf16[2,512,352]{1,2,0:T(8,128)(2,1)}, bf16[2,512,352]{1,2,0:T(8,128)(2,1)}, u32[]{:S(2)}, u32[]{:S(2)}) collective-permute-start(bf16[2,512,352]{1,2,0:T(8,128)(2,1)} %pad_maximum_fusion), channel_id=1, source_target_pairs={{0,12},{4,16},{8,20},{12,24},{16,28},{20,32},{24,36},{28,40},{32,4... | collective-permute-start | bytes 2162696 | tf_op jit(solution)/shard_map/ppermute | solution.py:16
  24.6 66.2 %collective-permute-start.2 = (bf16[2,512,352]{1,2,0:T(8,128)(2,1)}, bf16[2,512,352]{1,2,0:T(8,128)(2,1)}, u32[]{:S(2)}, u32[]{:S(2)}) collective-permute-start(bf16[2,512,352]{1,2,0:T(8,128)(2,1)} %pad_maximum_fusion), channel_id=1, source_target_pairs={{0,8},{4,12},{8,16},{12,20},{16,24},{20,28},{24,32},{28,36},{32,40... | collective-permute-start | bytes 2162696 | tf_op jit(solution)/shard_map/ppermute | solution.py:16
  27.9 65.6 %collective-permute-start.3 = (bf16[2,512,352]{1,2,0:T(8,128)(2,1)}, bf16[2,512,352]{1,2,0:T(8,128)(2,1)}, u32[]{:S(2)}, u32[]{:S(2)}) collective-permute-start(bf16[2,512,352]{1,2,0:T(8,128)(2,1)} %pad_maximum_fusion), channel_id=1, source_target_pairs={{0,4},{4,8},{8,12},{12,16},{16,20},{20,24},{24,28},{28,32},{32,36}... | collective-permute-start | bytes 2162696 | tf_op jit(solution)/shard_map/ppermute | solution.py:16
  29.8 65.0 %collective-permute-start.4 = (bf16[2,512,352]{1,2,0:T(8,128)(2,1)}, bf16[2,512,352]{1,2,0:T(8,128)(2,1)}, u32[]{:S(2)}, u32[]{:S(2)}) collective-permute-start(bf16[2,512,352]{1,2,0:T(8,128)(2,1)} %pad_maximum_fusion), channel_id=1, source_target_pairs={{4,0},{8,4},{12,8},{16,12},{20,16},{24,20},{28,24},{32,28},{36,32}... | collective-permute-start | bytes 2162696 | tf_op jit(solution)/shard_map/ppermute | solution.py:16
  85.7 8.9 %copy-start.6 = (bf16[1,512,352]{1,2,0:T(8,128)(2,1)S(1)}, bf16[1,512,352]{1,2,0:T(8,128)(2,1)}, u32[]{:S(2)}) copy-start(bf16[1,512,352]{1,2,0:T(8,128)(2,1)} %copy-done.5) | copy-start | bytes 1081348
  85.7 8.9 %copy-start.8 = (bf16[1,512,352]{1,2,0:T(8,128)(2,1)S(1)}, bf16[1,512,352]{1,2,0:T(8,128)(2,1)}, u32[]{:S(2)}) copy-start(bf16[1,512,352]{1,2,0:T(8,128)(2,1)} %copy-done.7) | copy-start | bytes 1081348
  85.8 17.2 %collective-permute-start.5 = (bf16[2,512,352]{1,2,0:T(8,128)(2,1)}, bf16[2,512,352]{1,2,0:T(8,128)(2,1)S(1)}, u32[]{:S(2)}, u32[]{:S(2)}) collective-permute-start(bf16[2,512,352]{1,2,0:T(8,128)(2,1)} %pad_maximum_fusion), channel_id=1, source_target_pairs={{8,0},{12,4},{16,8},{20,12},{24,16},{28,20},{32,24},{36,28},{40,32... | collective-permute-start | bytes 2162696 | tf_op jit(solution)/shard_map/ppermute | solution.py:16
  88.4 17.1 %collective-permute-start.6 = (bf16[2,512,352]{1,2,0:T(8,128)(2,1)}, bf16[2,512,352]{1,2,0:T(8,128)(2,1)S(1)}, u32[]{:S(2)}, u32[]{:S(2)}) collective-permute-start(bf16[2,512,352]{1,2,0:T(8,128)(2,1)} %pad_maximum_fusion), channel_id=1, source_target_pairs={{12,0},{16,4},{20,8},{24,12},{28,16},{32,20},{36,24},{40,28},{44,3... | collective-permute-start | bytes 2162696 | tf_op jit(solution)/shard_map/ppermute | solution.py:16
  90.8 24.8 %collective-permute-start.7 = (bf16[2,512,352]{1,2,0:T(8,128)(2,1)}, bf16[2,512,352]{1,2,0:T(8,128)(2,1)S(1)}, u32[]{:S(2)}, u32[]{:S(2)}) collective-permute-start(bf16[2,512,352]{1,2,0:T(8,128)(2,1)} %pad_maximum_fusion), channel_id=1, source_target_pairs={{16,0},{20,4},{24,8},{28,12},{32,16},{36,20},{40,24},{44,28},{48,3... | collective-permute-start | bytes 2162696 | tf_op jit(solution)/shard_map/ppermute | solution.py:16
  137.1 17.5 %copy-start.3 = (bf16[1,4608,352]{1,2,0:T(8,128)(2,1)S(1)}, bf16[1,4608,352]{1,2,0:T(8,128)(2,1)}, u32[]{:S(2)}) copy-start(bf16[1,4608,352]{1,2,0:T(8,128)(2,1)} %get-tuple-element.15) | copy-start | bytes 9732100
  169.8 96.6 %copy-start.2 = (bf16[512,1408]{1,0:T(8,128)(2,1)S(1)}, bf16[512,1408]{1,0:T(8,128)(2,1)}, u32[]{:S(2)}) copy-start(bf16[512,1408]{1,0:T(8,128)(2,1)} %param.13) | copy-start | bytes 4325380
  172.5 96.4 %copy-start.13 = (f32[1408]{0:T(1024)S(1)}, f32[1408]{0:T(1024)}, u32[]{:S(2)}) copy-start(f32[1408]{0:T(1024)} %param.21) | copy-start | bytes 16900
  172.5 184.1 %all-reduce.5.cloned.1.call-start = ((), (), s32[]{:S(2)}) async-start(), calls=%async_computation.3 | async-start | bytes 5767168 | tf_op jit(solution)/shard_map/psum | solution.py:32
  268.9 16.2 %copy-start.14 = (s32[32]{0:T(128)S(1)}, s32[32]{0:T(128)}, u32[]{:S(2)}) copy-start(s32[32]{0:T(128)} %param.15) | copy-start | bytes 388
  286.9 73.0 %copy-start.9 = (f32[1408]{0:T(1024)S(1)}, f32[1408]{0:T(1024)}, u32[]{:S(2)}) copy-start(f32[1408]{0:T(1024)} %param.24) | copy-start | bytes 16900
  370.6 16.3 %all-to-all-start = ((bf16[32,4,896]{2,1,0:T(4,128)(2,1)}), bf16[32,4,896]{2,1,0:T(4,128)(2,1)S(1)}, u32[]{:S(2)}, u32[]{:S(2)}) async-start(bf16[32,4,896]{2,1,0:T(4,128)(2,1)} %bitcast.46), calls=%async_computation | async-start | bytes 458752 | tf_op jit(solution)/shard_map/all_to_all | solution.py:63
  390.2 19.7 %all-to-all-start.1 = ((bf16[32,16,896]{2,1,0:T(8,128)(2,1)}), bf16[32,16,896]{2,1,0:T(8,128)(2,1)S(1)}, u32[]{:S(2)}, u32[]{:S(2)}) async-start(bf16[32,16,896]{2,1,0:T(8,128)(2,1)} %select_select_fusion), calls=%async_computation.1 | async-start | bytes 1835008 | tf_op jit(solution)/shard_map/all_to_all | solution.py:83
  393.9 17.8 %copy-start.1 = (bf16[352,1408]{1,0:T(8,128)(2,1)S(1)}, bf16[352,1408]{1,0:T(8,128)(2,1)}, u32[]{:S(2)}) copy-start(bf16[352,1408]{1,0:T(8,128)(2,1)} %param.20) | copy-start | bytes 2973700
Sparse Core Ops, SparseCore 0:
  172.6 93.8 all-reduce.2
  285.3 71.2 all-reduce.4
where the time goes:
time: 420 us; the launch traced here: 419 us
  waiting for transfers between devices  203 us (48%)
  matrix products  61.8 us (15%)
  blocking collectives  47.7 us (11%)
  other arithmetic  35.2 us (8%)
  starting transfers between devices  35 us (8%)
  local copies, waits for them, and re-layouts  20.4 us (5%)
  between operations  16 us (4%)
    psum x2, waiting for transfers between devices, sum_rows(): return lax.psum(partial_value, 'tp')  163 us
    psum x1, blocking collectives, shards(): counts = lax.psum(local_counts, 'seq')  47.7 us
    ppermute x8, starting transfers between devices, shifted(): lax.ppermute(value, axis, [(source, source + steps) for source in range(i...  23.2 us
    ppermute x8, waiting for transfers between devices, shifted(): lax.ppermute(value, axis, [(source, source + steps) for source in range(i...  19.6 us
    dot_general x1, matrix products, attend_window(): jnp.einsum('qhd,khd->hqk', query_heads, key_heads, preferred_element_type...  18.3 us
    reduce_sum x1, other arithmetic, attend_window(): row_total = jnp.sum(weights, axis=2)  17.4 us
    dot_general x1, matrix products, shards(): jnp.dot(hidden_units, down_weight, preferred_element_type=jnp.float32)  16.2 us
    dot_general x1, matrix products, attend_window(): jnp.einsum('hqk,khd->qhd', weights.astype(jnp.bfloat16), value_heads, pre...  15.3 us
  transfers between devices with their start and end apart: 12, of which 7 were waited for; matrix products, arithmetic and copies ran while one was open for 4% of the time, Pallas kernels for 0%

commit v1 on v0

--- a/solution.py
+++ b/solution.py
@@ -29,7 +29,7 @@
 
 
 def sum_rows(partial_value):
-    return lax.psum(partial_value, "tp")
+    return jnp.sum(lax.all_gather(partial_value, "tp"), axis=0)
 
 
 def attend_window(query_heads, key_heads, value_heads, query_image, key_image):

time: 420 us -> 512 us (1.22)
  waiting for transfers between devices: 203 us -> 280 us
  other arithmetic: 35.2 us -> 49.2 us
    all_gather x0 -> x2, waiting for transfers between devices: none -> 241 us  [sum_rows(): return jnp.sum(lax.all_gather(partial_value, 'tp'), axis=0)]
    psum x2 -> x0, waiting for transfers between devices: 163 us -> none  [sum_rows(): return lax.psum(partial_value, 'tp')]
    reduce_sum x0 -> x2, other arithmetic: none -> 14 us  [sum_rows(): return jnp.sum(lax.all_gather(partial_value, 'tp'), axis=0)]
  transfers between devices with their start and end apart: 12 -> 12, of which waited for: 7 -> 7; matrix products, arithmetic and copies ran while one was open for 4% -> 3% of each run, Pallas kernels for 0% -> 0%
where the time goes in v1:
time: 512 us; the launch traced here: 510 us
  waiting for transfers between devices  280 us (55%)
  matrix products  61.9 us (12%)
  other arithmetic  49.2 us (10%)
  blocking collectives  47.7 us (9%)
  starting transfers between devices  35 us (7%)
  local copies, waits for them, and re-layouts  20.4 us (4%)
  between operations  16 us (3%)
    all_gather x2, waiting for transfers between devices, sum_rows(): return jnp.sum(lax.all_gather(partial_value, 'tp'), axis=0)  241 us
    psum x1, blocking collectives, shards(): counts = lax.psum(local_counts, 'seq')  47.7 us
    ppermute x8, starting transfers between devices, shifted(): lax.ppermute(value, axis, [(source, source + steps) for source in range(i...  23.2 us
    ppermute x8, waiting for transfers between devices, shifted(): lax.ppermute(value, axis, [(source, source + steps) for source in range(i...  19.6 us
    dot_general x1, matrix products, attend_window(): jnp.einsum('qhd,khd->hqk', query_heads, key_heads, preferred_element_type...  18.3 us
    reduce_sum x1, other arithmetic, attend_window(): row_total = jnp.sum(weights, axis=2)  17.4 us
    dot_general x1, matrix products, shards(): jnp.dot(hidden_units, down_weight, preferred_element_type=jnp.float32)  16.2 us
    dot_general x1, matrix products, attend_window(): jnp.einsum('hqk,khd->qhd', weights.astype(jnp.bfloat16), value_heads, pre...  15.3 us
  transfers between devices with their start and end apart: 12, of which 7 were waited for; matrix products, arithmetic and copies ran while one was open for 3% of the time, Pallas kernels for 0%

profile of v1, /device:TPU:1, one launch (start us, length us, event | category | flops | bytes accessed | tf_op | source)
XLA Modules:
  0.0 510.4 jit_solution(5149023494728335813)
XLA Ops:
  6.5 2.0 convert_reduce_fusion
  8.6 1.9 fusion.18
  13.9 6.5 %collective-permute-start = (bf16[2,512,352]{1,2,0:T(8,128)(2,1)}, bf16[2,512,352]{1,2,0:T(8,128)(2,1)}, u32[]{:S(2)}, u32[]{:S(2)}) collective-permute-start(bf16[2,512,352]{1,2,0:T(8,128)(2,1)} %pad_maximum_fusion), channel_id=1, source_target_pairs={{0,16},{4,20},{8,24},{12,28},{16,32},{20,36},{24,40},{28,44},{32,4... | collective-permute-start | bytes 2162696 | tf_op jit(solution)/shard_map/ppermute | solution.py:16
  20.5 4.1 collective-permute-start.1
  24.6 3.2 collective-permute-start.2
  27.9 1.9 collective-permute-start.3
  29.8 3.2 collective-permute-start.4
  33.2 47.7 %psum.7 = s32[32]{0:T(128)S(1)} all-reduce(s32[32]{0:T(128)S(1)} %convert_reduce_fusion.2), channel_id=1, replica_groups=mesh['seq'=32,'tp'=4] {'seq'}, use_global_device_ids=true, to_apply=%region_1.0 | all-reduce | flops 32 | bytes 256 | tf_op jit(solution)/shard_map/psum | solution.py:114
  83.3 2.4 convolution_convert_fusion
  95.9 7.1 %collective-permute-done.5 = bf16[2,512,352]{1,2,0:T(8,128)(2,1)S(1)} collective-permute-done((bf16[2,512,352]{1,2,0:T(8,128)(2,1)}, bf16[2,512,352]{1,2,0:T(8,128)(2,1)S(1)}, u32[]{:S(2)}, u32[]{:S(2)}) %collective-permute-start.5) | collective-permute-done | bytes 720928 | tf_op jit(solution)/shard_map/ppermute | solution.py:16
  103.0 2.5 collective-permute-done.6
  105.5 10.1 %collective-permute-done.7 = bf16[2,512,352]{1,2,0:T(8,128)(2,1)S(1)} collective-permute-done((bf16[2,512,352]{1,2,0:T(8,128)(2,1)}, bf16[2,512,352]{1,2,0:T(8,128)(2,1)S(1)}, u32[]{:S(2)}, u32[]{:S(2)}) %collective-permute-start.7) | collective-permute-done | bytes 720928 | tf_op jit(solution)/shard_map/ppermute | solution.py:16
  115.7 3.1 fusion.112
  118.8 18.3 %fusion = (f32[4,512]{1,0:T(4,128)S(1)}, f32[4,512,4608]{2,1,0:T(8,128)}) fusion(pred[512,4608]{1,0:T(8,128)(4,1)S(1)} %broadcast_compare_fusion, bf16[512,4,88]{0,2,1:T(8,128)(2,1)S(1)} %bitcast.59, bf16[4608,4,88]{0,2,1:T(8,128)(2,1)} %bitcast.54), kind=kOutput, calls=%fused_computation.6 | convolution fusion | flops 1689253888 | bytes 43720704 | tf_op jit(solution)/shard_map/qhd,khd->hqk/dot_general | solution.py:36
  137.1 17.4 %fusion.1 = f32[4,512]{1,0:T(4,128)S(1)} fusion(f32[4,512,4608]{2,1,0:T(8,128)} %get-tuple-element.23, f32[4,512]{1,0:T(4,128)S(1)} %get-tuple-element.22, pred[512,4608]{1,0:T(8,128)(4,1)S(1)} %broadcast_compare_fusion), kind=kLoop, calls=%fused_computation.7 | loop fusion | flops 37746688 | bytes 40124416 | tf_op jit(solution)/shard_map/reduce_sum | solution.py:43
  154.6 15.3 %fusion.67 = bf16[512,4,88]{0,2,1:T(8,128)(2,1)S(1)} fusion(bf16[4608,4,88]{0,2,1:T(8,128)(2,1)S(1)} %bitcast.53, f32[4,512,4608]{2,1,0:T(8,128)} %get-tuple-element.23, f32[4,512]{1,0:T(4,128)S(1)} %get-tuple-element.22, pred[512,4608]{1,0:T(8,128)(4,1)S(1)} %broadcast_compare_fusion, f32[512,4]{0,1:T(4,128)S(1)} %bitcast.57), kind=kOutput, calls=%fused_computation.86 | convolution fusion | flops 1699053568 | bytes 43728896 | tf_op jit(solution)/shard_map/hqk,khd->qhd/dot_general | solution.py:44
  169.9 2.7 fusion.113
  172.8 132.0 %all-gather.5.cloned.1.call-done = f32[2048,1408]{1,0:T(8,128)} async-done(((f32[512,1408]{1,0:T(8,128)}), f32[2048,1408]{1,0:T(8,128)}) %all-gather.5.cloned.1.call-update) | async-done | bytes 11534352 | tf_op jit(solution)/shard_map/all_gather | solution.py:32
  304.8 7.0 %reduce_sum.127 = f32[512,1408]{1,0:T(8,128)} reduce(f32[4,512,1408]{2,1,0:T(8,128)} %bitcast.51, f32[]{:T(128)} %constant.63.clone.1), dimensions={0}, to_apply=%region_10.11 | reduce | flops 2162688 | bytes 14417924 | tf_op jit(solution)/shard_map/reduce_sum | solution.py:32
  311.8 2.4 fusion.71
  314.2 16.2 %fusion.20 = f32[512,1408]{1,0:T(8,128)} fusion(bf16[1536,1408]{1,0:T(8,128)(2,1)} %param.23, bf16[1408,1536]{1,0:T(8,128)(2,1)} %param.22, f32[1408]{0:T(1024)S(1)} %copy-done.13, f32[512]{0:T(512)S(1)} %get-tuple-element.19, f32[512]{0:T(512)S(1)} %get-tuple-element.18, f32[512,1408]{1,0:T(8,128)} %reduce_sum.127, bf16[512,1408]{1,0:T(8,128)(2,1)S(1)} %copy-done.2), kind=kOutput, calls=%fused_computation.43 | convolution fusion | flops 4484628480 | bytes 15869440 | tf_op jit(solution)/shard_map/dot_general | solution.py:153
  332.2 109.1 %all-gather.7.cloned.1.call-done = f32[2048,1408]{1,0:T(8,128)} async-done(((f32[512,1408]{1,0:T(8,128)}), f32[2048,1408]{1,0:T(8,128)}) %all-gather.7.cloned.1.call-update) | async-done | bytes 11534352 | tf_op jit(solution)/shard_map/all_gather | solution.py:32
  441.3 7.0 %reduce_sum.130 = f32[512,1408]{1,0:T(8,128)} reduce(f32[4,512,1408]{2,1,0:T(8,128)} %bitcast.50, f32[]{:T(128)} %constant.63.clone.1), dimensions={0}, to_apply=%region_13.14 | reduce | flops 2162688 | bytes 14417924 | tf_op jit(solution)/shard_map/reduce_sum | solution.py:32
  448.3 3.3 fusion.110
  451.7 1.6 multiply_convert_fusion
  453.2 2.7 reshape.342
  455.9 5.6 %convolution_convert_fusion.3 = bf16[128,896]{1,0:T(8,128)(2,1)S(1)} fusion(bf16[128,5632]{1,0:T(8,128)(2,1)S(1)} %reshape.342, bf16[5632,896]{1,0:T(8,128)(2,1)} %param.25), kind=kOutput, calls=%fused_computation.84 | convolution fusion | flops 1291960320 | bytes 11763712 | tf_op jit(solution)/shard_map/dot_general | solution.py:157
  462.3 7.7 %all-to-all-start = ((bf16[32,4,896]{2,1,0:T(4,128)(2,1)}), bf16[32,4,896]{2,1,0:T(4,128)(2,1)S(1)}, u32[]{:S(2)}, u32[]{:S(2)}) async-start(bf16[32,4,896]{2,1,0:T(4,128)(2,1)} %bitcast.48), calls=%async_computation | async-start | bytes 458752 | tf_op jit(solution)/shard_map/all_to_all | solution.py:63
  470.1 8.5 %all-to-all-done = bf16[32,4,896]{2,1,0:T(4,128)(2,1)S(1)} async-done(((bf16[32,4,896]{2,1,0:T(4,128)(2,1)}), bf16[32,4,896]{2,1,0:T(4,128)(2,1)S(1)}, u32[]{:S(2)}, u32[]{:S(2)}) %all-to-all-start) | async-done | bytes 229408 | tf_op jit(solution)/shard_map/all_to_all | solution.py:63
  478.6 2.1 gather_fusion.2
  481.9 3.8 all-to-all-start.1
  490.6 11.0 %all-to-all-done.1 = bf16[32,16,896]{2,1,0:T(8,128)(2,1)S(1)} async-done(((bf16[32,16,896]{2,1,0:T(8,128)(2,1)}), bf16[32,16,896]{2,1,0:T(8,128)(2,1)S(1)}, u32[]{:S(2)}, u32[]{:S(2)}) %all-to-all-start.1) | async-done | bytes 917536 | tf_op jit(solution)/shard_map/all_to_all | solution.py:83
  (93 shorter events, 25.1 us)
Async XLA Ops:
  6.5 163.3 %copy-start = (bf16[352,1408]{1,0:T(8,128)(2,1)S(1)}, bf16[352,1408]{1,0:T(8,128)(2,1)}, u32[]{:S(2)}) copy-start(bf16[352,1408]{1,0:T(8,128)(2,1)} %param.20) | copy-start | bytes 2973700
  6.5 3.9 copy-start.11
  6.5 298.3 %all-gather.5.cloned.1.call-start = ((), (), s32[]{:S(2)}) async-start(), calls=%async_computation.2 | async-start | bytes 14417920 | tf_op jit(solution)/shard_map/all_gather | solution.py:32
  10.5 2.5 copy-start.4
  10.5 1.7 copy-start.12
  12.2 1.8 copy-start.5
  12.2 20.9 %copy-start.10 = (s32[128]{0:T(128)S(1)}, s32[128]{0:T(128)}, u32[]{:S(2)}) copy-start(s32[128]{0:T(128)} %param.14) | copy-start | bytes 1540
  13.0 7.5 %copy-start.7 = (bf16[1,512,352]{1,2,0:T(8,128)(2,1)}, bf16[1,512,352]{1,2,0:T(8,128)(2,1)S(1)}, u32[]{:S(2)}) copy-start(bf16[1,512,352]{1,2,0:T(8,128)(2,1)S(1)} %fusion.62) | copy-start | bytes 1081348
  13.9 71.8 %collective-permute-start = (bf16[2,512,352]{1,2,0:T(8,128)(2,1)}, bf16[2,512,352]{1,2,0:T(8,128)(2,1)}, u32[]{:S(2)}, u32[]{:S(2)}) collective-permute-start(bf16[2,512,352]{1,2,0:T(8,128)(2,1)} %pad_maximum_fusion), channel_id=1, source_target_pairs={{0,16},{4,20},{8,24},{12,28},{16,32},{20,36},{24,40},{28,44},{32,4... | collective-permute-start | bytes 2162696 | tf_op jit(solution)/shard_map/ppermute | solution.py:16
  20.5 67.9 %collective-permute-start.1 = (bf16[2,512,352]{1,2,0:T(8,128)(2,1)}, bf16[2,512,352]{1,2,0:T(8,128)(2,1)}, u32[]{:S(2)}, u32[]{:S(2)}) collective-permute-start(bf16[2,512,352]{1,2,0:T(8,128)(2,1)} %pad_maximum_fusion), channel_id=1, source_target_pairs={{0,12},{4,16},{8,20},{12,24},{16,28},{20,32},{24,36},{28,40},{32,4... | collective-permute-start | bytes 2162696 | tf_op jit(solution)/shard_map/ppermute | solution.py:16
  24.6 66.2 %collective-permute-start.2 = (bf16[2,512,352]{1,2,0:T(8,128)(2,1)}, bf16[2,512,352]{1,2,0:T(8,128)(2,1)}, u32[]{:S(2)}, u32[]{:S(2)}) collective-permute-start(bf16[2,512,352]{1,2,0:T(8,128)(2,1)} %pad_maximum_fusion), channel_id=1, source_target_pairs={{0,8},{4,12},{8,16},{12,20},{16,24},{20,28},{24,32},{28,36},{32,40... | collective-permute-start | bytes 2162696 | tf_op jit(solution)/shard_map/ppermute | solution.py:16
  27.9 65.6 %collective-permute-start.3 = (bf16[2,512,352]{1,2,0:T(8,128)(2,1)}, bf16[2,512,352]{1,2,0:T(8,128)(2,1)}, u32[]{:S(2)}, u32[]{:S(2)}) collective-permute-start(bf16[2,512,352]{1,2,0:T(8,128)(2,1)} %pad_maximum_fusion), channel_id=1, source_target_pairs={{0,4},{4,8},{8,12},{12,16},{16,20},{20,24},{24,28},{28,32},{32,36}... | collective-permute-start | bytes 2162696 | tf_op jit(solution)/shard_map/ppermute | solution.py:16
  29.8 65.0 %collective-permute-start.4 = (bf16[2,512,352]{1,2,0:T(8,128)(2,1)}, bf16[2,512,352]{1,2,0:T(8,128)(2,1)}, u32[]{:S(2)}, u32[]{:S(2)}) collective-permute-start(bf16[2,512,352]{1,2,0:T(8,128)(2,1)} %pad_maximum_fusion), channel_id=1, source_target_pairs={{4,0},{8,4},{12,8},{16,12},{20,16},{24,20},{28,24},{32,28},{36,32}... | collective-permute-start | bytes 2162696 | tf_op jit(solution)/shard_map/ppermute | solution.py:16
  85.7 8.9 %copy-start.6 = (bf16[1,512,352]{1,2,0:T(8,128)(2,1)S(1)}, bf16[1,512,352]{1,2,0:T(8,128)(2,1)}, u32[]{:S(2)}) copy-start(bf16[1,512,352]{1,2,0:T(8,128)(2,1)} %copy-done.5) | copy-start | bytes 1081348
  85.7 8.9 %copy-start.8 = (bf16[1,512,352]{1,2,0:T(8,128)(2,1)S(1)}, bf16[1,512,352]{1,2,0:T(8,128)(2,1)}, u32[]{:S(2)}) copy-start(bf16[1,512,352]{1,2,0:T(8,128)(2,1)} %copy-done.7) | copy-start | bytes 1081348
  85.8 17.2 %collective-permute-start.5 = (bf16[2,512,352]{1,2,0:T(8,128)(2,1)}, bf16[2,512,352]{1,2,0:T(8,128)(2,1)S(1)}, u32[]{:S(2)}, u32[]{:S(2)}) collective-permute-start(bf16[2,512,352]{1,2,0:T(8,128)(2,1)} %pad_maximum_fusion), channel_id=1, source_target_pairs={{8,0},{12,4},{16,8},{20,12},{24,16},{28,20},{32,24},{36,28},{40,32... | collective-permute-start | bytes 2162696 | tf_op jit(solution)/shard_map/ppermute | solution.py:16
  88.4 17.1 %collective-permute-start.6 = (bf16[2,512,352]{1,2,0:T(8,128)(2,1)}, bf16[2,512,352]{1,2,0:T(8,128)(2,1)S(1)}, u32[]{:S(2)}, u32[]{:S(2)}) collective-permute-start(bf16[2,512,352]{1,2,0:T(8,128)(2,1)} %pad_maximum_fusion), channel_id=1, source_target_pairs={{12,0},{16,4},{20,8},{24,12},{28,16},{32,20},{36,24},{40,28},{44,3... | collective-permute-start | bytes 2162696 | tf_op jit(solution)/shard_map/ppermute | solution.py:16
  90.8 24.8 %collective-permute-start.7 = (bf16[2,512,352]{1,2,0:T(8,128)(2,1)}, bf16[2,512,352]{1,2,0:T(8,128)(2,1)S(1)}, u32[]{:S(2)}, u32[]{:S(2)}) collective-permute-start(bf16[2,512,352]{1,2,0:T(8,128)(2,1)} %pad_maximum_fusion), channel_id=1, source_target_pairs={{16,0},{20,4},{24,8},{28,12},{32,16},{36,20},{40,24},{44,28},{48,3... | collective-permute-start | bytes 2162696 | tf_op jit(solution)/shard_map/ppermute | solution.py:16
  137.1 17.5 %copy-start.3 = (bf16[1,4608,352]{1,2,0:T(8,128)(2,1)S(1)}, bf16[1,4608,352]{1,2,0:T(8,128)(2,1)}, u32[]{:S(2)}) copy-start(bf16[1,4608,352]{1,2,0:T(8,128)(2,1)} %get-tuple-element.15) | copy-start | bytes 9732100
  172.5 268.7 %all-gather.7.cloned.1.call-start = ((), (), s32[]{:S(2)}) async-start(), calls=%async_computation.3 | async-start | bytes 14417920 | tf_op jit(solution)/shard_map/all_gather | solution.py:32
  304.8 7.0 %copy-start.2 = (bf16[512,1408]{1,0:T(8,128)(2,1)S(1)}, bf16[512,1408]{1,0:T(8,128)(2,1)}, u32[]{:S(2)}) copy-start(bf16[512,1408]{1,0:T(8,128)(2,1)} %param.13) | copy-start | bytes 4325380
  311.8 2.4 copy-start.13
  314.2 16.2 %copy-start.14 = (s32[32]{0:T(128)S(1)}, s32[32]{0:T(128)}, u32[]{:S(2)}) copy-start(s32[32]{0:T(128)} %param.15) | copy-start | bytes 388
  448.3 3.4 copy-start.9
  462.3 16.3 %all-to-all-start = ((bf16[32,4,896]{2,1,0:T(4,128)(2,1)}), bf16[32,4,896]{2,1,0:T(4,128)(2,1)S(1)}, u32[]{:S(2)}, u32[]{:S(2)}) async-start(bf16[32,4,896]{2,1,0:T(4,128)(2,1)} %bitcast.48), calls=%async_computation | async-start | bytes 458752 | tf_op jit(solution)/shard_map/all_to_all | solution.py:63
  481.9 19.7 %all-to-all-start.1 = ((bf16[32,16,896]{2,1,0:T(8,128)(2,1)}), bf16[32,16,896]{2,1,0:T(8,128)(2,1)S(1)}, u32[]{:S(2)}, u32[]{:S(2)}) async-start(bf16[32,16,896]{2,1,0:T(8,128)(2,1)} %select_select_fusion), calls=%async_computation.1 | async-start | bytes 1835008 | tf_op jit(solution)/shard_map/all_to_all | solution.py:83
  485.7 17.8 %copy-start.1 = (bf16[352,1408]{1,0:T(8,128)(2,1)S(1)}, bf16[352,1408]{1,0:T(8,128)(2,1)}, u32[]{:S(2)}) copy-start(bf16[352,1408]{1,0:T(8,128)(2,1)} %param.20) | copy-start | bytes 2973700
Sparse Core Ops, SparseCore 0:
  172.7 132.0 all-gather.4
  330.5 110.6 all-gather.6
